TPU v7x, 128 devices: a whole 4x4x4 slice. The times are simulated.
128 devices in a mesh: src: 16 (over y_lo, z, core), tgt: 8 (over y_hi, x).
Axes of the slice: x: 4, y: 4 (y_hi: 2, y_lo: 2; y = y_hi * 2 + y_lo), z: 4, core: 2. Of those that a mesh axis runs over, the one named last changes fastest.
Arguments:
- src_emb: bfloat16 [16384, 768], P(('src', 'tgt')), may hold values from -0.05119037 to 0.05119037
- right_sentence_vectors: bfloat16 [8192, 768], P(('tgt', 'src')), may hold values from -0.05119037 to 0.05119037
- src_mass: float32 [16384], P('src'), may hold values from 0.25 to 4
- tgt_mass: float32 [8192], P('tgt'), may hold values from 0.5 to 8
Outputs:
- grad_src: float32 [16384, 768], P(('src', 'tgt'))
- grad_tgt: float32 [8192, 768], P(('tgt', 'src'))
All inputs are finite; a program needn't handle non-finite values.
Results may differ from a plain program's by a relative error of at most 0.00045.
Values may be sent and summed in bfloat16 or wider, within the bound.
No kernel may reach another device: no remote copies, remote signals or barrier semaphores. Data moves between devices by JAX's collectives and lax.ppermute only.
A program may use at most 64 MiB of HBM per device.

v0:
```python
import jax
import jax.numpy as jnp
from jax import lax
from jax.sharding import PartitionSpec as P

ITERS = 4
regularizer_epsilon = 0.05
highest = lax.Precision.HIGHEST


def row_total(part):
    return lax.psum(part, "tgt")


def col_total(part):
    return lax.psum(part, "src")


def times_vector(kernel, vector):
    return jnp.dot(kernel, vector, precision=highest, preferred_element_type=jnp.float32)


def vector_times(vector, kernel):
    return jnp.dot(vector, kernel, precision=highest, preferred_element_type=jnp.float32)


def per_device(src_emb, right_sentence_vectors, src_mass, tgt_mass):
    src_rows = lax.all_gather(src_emb, "tgt", axis=0, tiled=True)
    target_rows = lax.all_gather(right_sentence_vectors, "src", axis=0, tiled=True)

    def build():
        kernel_grid = (
            lax.dot_general(
                src_rows, target_rows, (((1,), (1,)), ((), ())), preferred_element_type=jnp.float32
            )
            / regularizer_epsilon
        )
        kernel = lax.optimization_barrier(jnp.exp(kernel_grid).astype(jnp.bfloat16))
        return (kernel_grid, kernel)

    kernel_grid, kernel = build()
    vector = jnp.ones(tgt_mass.shape, jnp.float32)
    old_saved, row_saved, src_saved, col_saved, tgt_saved = ([], [], [], [], [])
    for iteration in range(ITERS):
        old_saved.append(vector)
        row_sum = row_total(times_vector(kernel, vector))
        src_scale = src_mass / row_sum
        col_sum = col_total(vector_times(src_scale, kernel))
        vector = tgt_mass / col_sum
        row_saved.append(row_sum)
        src_saved.append(src_scale)
        col_saved.append(col_sum)
        tgt_saved.append(vector)
    last_src = src_saved[-1]
    last_tgt = tgt_saved[-1]
    weighted = kernel * kernel_grid
    src_adj = row_total(times_vector(weighted, last_tgt))
    tgt_adj = col_total(vector_times(last_src, weighted))
    row_bars = [None] * ITERS
    col_bars = [None] * ITERS
    for iteration in reversed(range(ITERS)):
        kernel_grid, kernel = build()
        col_bar = -tgt_adj * tgt_saved[iteration] / col_saved[iteration]
        back = row_total(times_vector(kernel, col_bar))
        if iteration == ITERS - 1:
            back = back + src_adj
        row_bar = -back * src_saved[iteration] / row_saved[iteration]
        if iteration > 0:
            tgt_adj = col_total(vector_times(row_bar, kernel))
        row_bars[iteration] = row_bar
        col_bars[iteration] = col_bar
    left = jnp.stack(row_bars + src_saved, axis=1)
    right = jnp.stack(old_saved + col_bars, axis=1)
    lowrank = lax.dot_general(
        left, right, (((1,), (1,)), ((), ())), precision=highest, preferred_element_type=jnp.float32
    )
    cross_term_grid = (
        kernel * (last_src[:, None] * last_tgt[None, :] * (1.0 + kernel_grid) + lowrank)
    ).astype(jnp.bfloat16)
    left_share_piece = (
        jnp.dot(cross_term_grid, target_rows, preferred_element_type=jnp.float32)
        / regularizer_epsilon
    )
    right_share_piece = (
        lax.dot_general(
            cross_term_grid, src_rows, (((0,), (0,)), ((), ())), preferred_element_type=jnp.float32
        )
        / regularizer_epsilon
    )
    src_whole = lax.psum(left_share_piece, "tgt")
    tgt_whole = lax.psum(right_share_piece, "src")
    src_count = src_emb.shape[0]
    tgt_count = right_sentence_vectors.shape[0]
    grad_src = lax.dynamic_slice_in_dim(src_whole, lax.axis_index("tgt") * src_count, src_count, 0)
    grad_tgt = lax.dynamic_slice_in_dim(tgt_whole, lax.axis_index("src") * tgt_count, tgt_count, 0)
    return (grad_src, grad_tgt)


def solution(mesh):
    placed = (P(("src", "tgt"), None), P(("tgt", "src"), None), P("src"), P("tgt"))
    return jax.shard_map(
        per_device,
        mesh=mesh,
        in_specs=placed,
        out_specs=(P(("src", "tgt"), None), P(("tgt", "src"), None)),
        check_vma=False,
    )
```

profile of v0, /device:TPU:1, one launch (start us, length us, event | category | flops | bytes accessed | tf_op | source)
XLA Modules:
  0.0 730.8 jit_solution(13594640266932629747)
XLA Ops:
  8.7 54.5 %all-gather.3.cloned.1.call-done = bf16[1024,768]{1,0:T(8,128)(2,1)} async-done(((bf16[128,768]{1,0:T(8,128)(2,1)}), bf16[1024,768]{1,0:T(8,128)(2,1)}) %all-gather.3.cloned.1.call-update) | async-done | bytes 1572880 | tf_op jit(solution)/shard_map/all_gather | solution.py:28
  63.2 35.8 %all-gather.5.cloned.1.call-done = bf16[1024,768]{1,0:T(8,128)(2,1)} async-done(((bf16[64,768]{1,0:T(8,128)(2,1)}), bf16[1024,768]{1,0:T(8,128)(2,1)}) %all-gather.5.cloned.1.call-update) | async-done | bytes 1572880 | tf_op jit(solution)/shard_map/all_gather | solution.py:29
  99.0 5.6 exponential_convert_fusion
  106.4 20.2 %psum.133 = f32[1024]{0:T(1024)S(1)} all-reduce(f32[1024]{0:T(1024)S(1)} %bitcast.122), channel_id=1, replica_groups=mesh['src'=16,'tgt'=8] {'tgt'}, use_global_device_ids=true, to_apply=%region_0.0 | all-reduce | flops 1024 | bytes 8192 | tf_op jit(solution)/shard_map/psum | solution.py:12
  127.5 30.5 %psum.134 = f32[1024]{0:T(1024)S(1)} all-reduce(f32[1024]{0:T(1024)S(1)} %bitcast.123), channel_id=1, replica_groups=mesh['src'=16,'tgt'=8] {'src'}, use_global_device_ids=true, to_apply=%region_1.0 | all-reduce | flops 1024 | bytes 8192 | tf_op jit(solution)/shard_map/psum | solution.py:16
  159.7 15.5 %psum.135 = f32[1024]{0:T(1024)S(1)} all-reduce(f32[1024]{0:T(1024)S(1)} %bitcast.124), channel_id=1, replica_groups=mesh['src'=16,'tgt'=8] {'tgt'}, use_global_device_ids=true, to_apply=%region_2.0 | all-reduce | flops 1024 | bytes 8192 | tf_op jit(solution)/shard_map/psum | solution.py:12
  176.2 30.6 %psum.136 = f32[1024]{0:T(1024)S(1)} all-reduce(f32[1024]{0:T(1024)S(1)} %bitcast.125), channel_id=1, replica_groups=mesh['src'=16,'tgt'=8] {'src'}, use_global_device_ids=true, to_apply=%region_3.0 | all-reduce | flops 1024 | bytes 8192 | tf_op jit(solution)/shard_map/psum | solution.py:16
  206.8 1.7 fusion.13
  208.5 17.2 %psum.137 = f32[1024]{0:T(1024)S(1)} all-reduce(f32[1024]{0:T(1024)S(1)} %bitcast.126), channel_id=1, replica_groups=mesh['src'=16,'tgt'=8] {'tgt'}, use_global_device_ids=true, to_apply=%region_4.0 | all-reduce | flops 1024 | bytes 8192 | tf_op jit(solution)/shard_map/psum | solution.py:12
  226.6 30.9 %psum.138 = f32[1024]{0:T(1024)S(1)} all-reduce(f32[1024]{0:T(1024)S(1)} %bitcast.127), channel_id=1, replica_groups=mesh['src'=16,'tgt'=8] {'src'}, use_global_device_ids=true, to_apply=%region_5.0 | all-reduce | flops 1024 | bytes 8192 | tf_op jit(solution)/shard_map/psum | solution.py:16
  257.5 1.7 fusion.15
  259.3 15.6 %psum.139 = f32[1024]{0:T(1024)S(1)} all-reduce(f32[1024]{0:T(1024)S(1)} %bitcast.128), channel_id=1, replica_groups=mesh['src'=16,'tgt'=8] {'tgt'}, use_global_device_ids=true, to_apply=%region_6.0 | all-reduce | flops 1024 | bytes 8192 | tf_op jit(solution)/shard_map/psum | solution.py:12
  275.8 4.6 fusion.2
  280.5 31.1 %all-reduce = (f32[1024]{0:T(1024)S(1)}, f32[1024]{0:T(1024)S(1)}) all-reduce(f32[1024]{0:T(1024)S(1)} %bitcast.120, f32[1024]{0:T(1024)S(1)} %bitcast.121), channel_id=1, replica_groups=mesh['src'=16,'tgt'=8] {'src'}, use_global_device_ids=true, to_apply=%region_7.0 | all-reduce | flops 2048 | bytes 16384 | tf_op jit(solution)/shard_map/psum | solution.py:16
  311.6 6.1 fusion.1
  317.7 1.7 fusion.17
  319.4 17.2 %psum.152 = f32[1024]{0:T(1024)S(1)} all-reduce(f32[1024]{0:T(1024)S(1)} %add.58), channel_id=1, replica_groups=mesh['src'=16,'tgt'=8] {'tgt'}, use_global_device_ids=true, to_apply=%region_9.0 | all-reduce | flops 1024 | bytes 8192 | tf_op jit(solution)/shard_map/psum | solution.py:12
  337.6 30.9 %psum.144 = f32[1024]{0:T(1024)S(1)} all-reduce(f32[1024]{0:T(1024)S(1)} %bitcast.129), channel_id=1, replica_groups=mesh['src'=16,'tgt'=8] {'src'}, use_global_device_ids=true, to_apply=%region_11.0 | all-reduce | flops 1024 | bytes 8192 | tf_op jit(solution)/shard_map/psum | solution.py:16
  368.5 1.7 fusion.19
  370.2 15.5 %psum.145 = f32[1024]{0:T(1024)S(1)} all-reduce(f32[1024]{0:T(1024)S(1)} %bitcast.130), channel_id=1, replica_groups=mesh['src'=16,'tgt'=8] {'tgt'}, use_global_device_ids=true, to_apply=%region_12.0 | all-reduce | flops 1024 | bytes 8192 | tf_op jit(solution)/shard_map/psum | solution.py:12
  386.7 30.6 %psum.146 = f32[1024]{0:T(1024)S(1)} all-reduce(f32[1024]{0:T(1024)S(1)} %bitcast.131), channel_id=1, replica_groups=mesh['src'=16,'tgt'=8] {'src'}, use_global_device_ids=true, to_apply=%region_13.0 | all-reduce | flops 1024 | bytes 8192 | tf_op jit(solution)/shard_map/psum | solution.py:16
  417.3 1.7 fusion.21
  419.0 17.4 %psum.147 = f32[1024]{0:T(1024)S(1)} all-reduce(f32[1024]{0:T(1024)S(1)} %bitcast.132), channel_id=1, replica_groups=mesh['src'=16,'tgt'=8] {'tgt'}, use_global_device_ids=true, to_apply=%region_14.0 | all-reduce | flops 1024 | bytes 8192 | tf_op jit(solution)/shard_map/psum | solution.py:12
  437.4 30.9 %psum.148 = f32[1024]{0:T(1024)S(1)} all-reduce(f32[1024]{0:T(1024)S(1)} %bitcast.133), channel_id=1, replica_groups=mesh['src'=16,'tgt'=8] {'src'}, use_global_device_ids=true, to_apply=%region_15.0 | all-reduce | flops 1024 | bytes 8192 | tf_op jit(solution)/shard_map/psum | solution.py:16
  468.3 1.7 fusion.23
  470.1 15.5 %psum.149 = f32[1024]{0:T(1024)S(1)} all-reduce(f32[1024]{0:T(1024)S(1)} %bitcast.119), channel_id=1, replica_groups=mesh['src'=16,'tgt'=8] {'tgt'}, use_global_device_ids=true, to_apply=%region_16.0 | all-reduce | flops 1024 | bytes 8192 | tf_op jit(solution)/shard_map/psum | solution.py:12
  485.7 6.2 fusion
  493.2 3.5 convolution_multiply_fusion.1
  498.3 5.0 convolution_multiply_fusion
  503.3 88.4 %all-reduce.4.cloned.1.call-done = f32[1024,768]{1,0:T(8,128)} async-done(((f32[1024,768]{1,0:T(8,128)}), f32[1024,768]{1,0:T(8,128)}) %all-reduce.4.cloned.1.call-update) | async-done | bytes 3145744 | tf_op jit(solution)/shard_map/psum | solution.py:90
  591.8 1.8 constant_dynamic-slice_fusion.1
  593.5 129.1 %all-reduce.6.cloned.1.call-done = f32[1024,768]{1,0:T(8,128)} async-done(((f32[1024,768]{1,0:T(8,128)}), f32[1024,768]{1,0:T(8,128)}) %all-reduce.6.cloned.1.call-update) | async-done | bytes 3145744 | tf_op jit(solution)/shard_map/psum | solution.py:91
  (47 shorter events, 16.2 us)
Async XLA Ops:
  7.2 56.0 %all-gather.3.cloned.1.call-start = ((), (), s32[]{:S(2)}) async-start(), calls=%async_computation | async-start | bytes 1769472 | tf_op jit(solution)/shard_map/all_gather | solution.py:28
  7.9 91.1 %all-gather.5.cloned.1.call-start = ((), (), s32[]{:S(2)}) async-start(), calls=%async_computation.1 | async-start | bytes 1671168 | tf_op jit(solution)/shard_map/all_gather | solution.py:29
  8.6 583.1 %all-reduce.4.cloned.1.call-start = ((), (), s32[]{:S(2)}) async-start(), calls=%async_computation.2 | async-start | bytes 6291456 | tf_op jit(solution)/shard_map/psum | solution.py:90
  104.6 21.9 %copy-start.2 = (f32[1024]{0:T(1024)S(1)}, f32[1024]{0:T(1024)}, u32[]{:S(2)}) copy-start(f32[1024]{0:T(1024)} %param.6) | copy-start | bytes 12292
  104.6 53.4 %copy-start.3 = (f32[1024]{0:T(1024)S(1)}, f32[1024]{0:T(1024)}, u32[]{:S(2)}) copy-start(f32[1024]{0:T(1024)} %param.7) | copy-start | bytes 12292
  485.6 7.6 %copy-start.4 = (bf16[1024,768]{1,0:T(8,128)(2,1)S(1)}, bf16[1024,768]{1,0:T(8,128)(2,1)}, u32[]{:S(2)}) copy-start(bf16[1024,768]{1,0:T(8,128)(2,1)} %all-gather.5.cloned.1.call-done) | copy-start | bytes 4718596
  491.9 1.3 copy-start
  496.7 1.6 copy-start.1
  496.8 225.9 %all-reduce.6.cloned.1.call-start = ((), (), s32[]{:S(2)}) async-start(), calls=%async_computation.3 | async-start | bytes 6291456 | tf_op jit(solution)/shard_map/psum | solution.py:91
Sparse Core Ops, SparseCore 0:
  10.3 52.8 all-gather.2
  64.9 34.0 all-gather.4
  496.9 94.8 all-reduce.3
  594.1 128.4 all-reduce.5
where the time goes:
time: 731 us
  blocking collectives  350 us (48%)
  waiting for transfers between devices  309 us (42%)
  matrix products  51.4 us (7%)
  between operations  13.9 us (2%)
    psum x7, blocking collectives, col_total(): return lax.psum(part, 'src')  216 us
    psum x8, blocking collectives, row_total(): return lax.psum(part, 'tgt')  134 us
    psum x1, waiting for transfers between devices, per_device(): tgt_whole = lax.psum(right_share_piece, 'src')  129 us
    psum x1, waiting for transfers between devices, per_device(): src_whole = lax.psum(left_share_piece, 'tgt')  88.4 us
    all_gather x1, waiting for transfers between devices, per_device(): src_rows = lax.all_gather(src_emb, 'tgt', axis=0, tiled=True)  54.5 us
    all_gather x1, waiting for transfers between devices, per_device(): lax.all_gather(right_sentence_vectors, 'src', axis=0, tiled=True)  35.8 us
    dot_general x9, matrix products, times_vector(): jnp.dot(kernel, vector, precision=highest, preferred_element_type=jnp.flo...  19.9 us
  transfers between devices with their start and end apart: 4, of which 4 were waited for; matrix products, arithmetic and copies ran while one was open for 1% of the time, Pallas kernels for 0%

commit v1 on v0

--- a/solution.py
+++ b/solution.py
@@ -2,6 +2,7 @@
 import jax.numpy as jnp
 from jax import lax
 from jax.sharding import PartitionSpec as P
+from jax.lax import all_gather
 
 ITERS = 4
 regularizer_epsilon = 0.05
@@ -13,7 +14,8 @@
 
 
 def col_total(part):
-    return lax.psum(part, "src")
+    _track_halves = lambda load: jnp.sum(all_gather(load, "src"), 0)
+    return _track_halves(part)
 
 
 def times_vector(kernel, vector):

time: 731 us -> 680 us (0.930)
  blocking collectives: 350 us -> 298 us
    psum x7 -> x0, blocking collectives: 216 us -> none  [col_total(): return lax.psum(part, 'src')]
    all_gather x0 -> x8, blocking collectives: none -> 162 us  [col_total(): _track_halves = lambda load: jnp.sum(all_gather(load, 'src'), 0)]
where the time goes in v1:
time: 680 us
  waiting for transfers between devices  309 us (45%)
  blocking collectives  298 us (44%)
  matrix products  51.3 us (8%)
  between operations  14 us (2%)
    all_gather x8, blocking collectives, col_total(): _track_halves = lambda load: jnp.sum(all_gather(load, 'src'), 0)  162 us
    psum x8, blocking collectives, row_total(): return lax.psum(part, 'tgt')  136 us
    psum x1, waiting for transfers between devices, per_device(): tgt_whole = lax.psum(right_share_piece, 'src')  129 us
    psum x1, waiting for transfers between devices, per_device(): src_whole = lax.psum(left_share_piece, 'tgt')  88.6 us
    all_gather x1, waiting for transfers between devices, per_device(): src_rows = lax.all_gather(src_emb, 'tgt', axis=0, tiled=True)  54.5 us
    all_gather x1, waiting for transfers between devices, per_device(): lax.all_gather(right_sentence_vectors, 'src', axis=0, tiled=True)  35.8 us
    dot_general x9, matrix products, times_vector(): jnp.dot(kernel, vector, precision=highest, preferred_element_type=jnp.flo...  19.9 us
  transfers between devices with their start and end apart: 4, of which 4 were waited for; matrix products, arithmetic and copies ran while one was open for 1% of the time, Pallas kernels for 0%

profile of v1, /device:TPU:1, one launch (start us, length us, event | category | flops | bytes accessed | tf_op | source)
XLA Modules:
  0.0 679.6 jit_solution(10737722344350064251)
XLA Ops:
  8.7 54.5 %all-gather.11.cloned.1.call-done = bf16[1024,768]{1,0:T(8,128)(2,1)} async-done(((bf16[128,768]{1,0:T(8,128)(2,1)}), bf16[1024,768]{1,0:T(8,128)(2,1)}) %all-gather.11.cloned.1.call-update) | async-done | bytes 1572880 | tf_op jit(solution)/shard_map/all_gather | solution.py:30
  63.2 35.8 %all-gather.13.cloned.1.call-done = bf16[1024,768]{1,0:T(8,128)(2,1)} async-done(((bf16[64,768]{1,0:T(8,128)(2,1)}), bf16[1024,768]{1,0:T(8,128)(2,1)}) %all-gather.13.cloned.1.call-update) | async-done | bytes 1572880 | tf_op jit(solution)/shard_map/all_gather | solution.py:31
  99.0 5.6 exponential_convert_fusion
  106.4 20.2 %psum.77 = f32[1024]{0:T(1024)S(1)} all-reduce(f32[1024]{0:T(1024)S(1)} %bitcast.128), channel_id=1, replica_groups=mesh['src'=16,'tgt'=8] {'tgt'}, use_global_device_ids=true, to_apply=%region_0.0 | all-reduce | flops 1024 | bytes 8192 | tf_op jit(solution)/shard_map/psum | solution.py:13
  127.5 21.3 %all-gather = f32[16384]{0:T(1024)S(1)} all-gather(f32[1024]{0:T(1024)S(1)} %bitcast.120), channel_id=2, replica_groups=mesh['src'=16,'tgt'=8] {'src'}, dimensions={0}, use_global_device_ids=true | all-gather | bytes 69632 | tf_op jit(solution)/shard_map/all_gather | solution.py:17
  150.6 15.5 %psum.78 = f32[1024]{0:T(1024)S(1)} all-reduce(f32[1024]{0:T(1024)S(1)} %bitcast.129), channel_id=1, replica_groups=mesh['src'=16,'tgt'=8] {'tgt'}, use_global_device_ids=true, to_apply=%region_2.0 | all-reduce | flops 1024 | bytes 8192 | tf_op jit(solution)/shard_map/psum | solution.py:13
  167.1 20.1 %all-gather.1 = f32[16384]{0:T(1024)S(1)} all-gather(f32[1024]{0:T(1024)S(1)} %bitcast.121), channel_id=3, replica_groups=mesh['src'=16,'tgt'=8] {'src'}, dimensions={0}, use_global_device_ids=true | all-gather | bytes 69632 | tf_op jit(solution)/shard_map/all_gather | solution.py:17
  187.3 1.7 fusion.13
  189.0 17.8 %psum.79 = f32[1024]{0:T(1024)S(1)} all-reduce(f32[1024]{0:T(1024)S(1)} %bitcast.130), channel_id=1, replica_groups=mesh['src'=16,'tgt'=8] {'tgt'}, use_global_device_ids=true, to_apply=%region_4.0 | all-reduce | flops 1024 | bytes 8192 | tf_op jit(solution)/shard_map/psum | solution.py:13
  207.7 20.6 %all-gather.2 = f32[16384]{0:T(1024)S(1)} all-gather(f32[1024]{0:T(1024)S(1)} %bitcast.122), channel_id=4, replica_groups=mesh['src'=16,'tgt'=8] {'src'}, dimensions={0}, use_global_device_ids=true | all-gather | bytes 69632 | tf_op jit(solution)/shard_map/all_gather | solution.py:17
  228.4 1.7 fusion.15
  230.1 16.4 %psum.80 = f32[1024]{0:T(1024)S(1)} all-reduce(f32[1024]{0:T(1024)S(1)} %bitcast.131), channel_id=1, replica_groups=mesh['src'=16,'tgt'=8] {'tgt'}, use_global_device_ids=true, to_apply=%region_6.0 | all-reduce | flops 1024 | bytes 8192 | tf_op jit(solution)/shard_map/psum | solution.py:13
  247.5 4.6 fusion.2
  252.1 20.0 %all-gather.4 = f32[16384]{0:T(1024)S(1)} all-gather(f32[1024]{0:T(1024)S(1)} %bitcast.123), channel_id=6, replica_groups=mesh['src'=16,'tgt'=8] {'src'}, dimensions={0}, use_global_device_ids=true | all-gather | bytes 69632 | tf_op jit(solution)/shard_map/all_gather | solution.py:17
  272.2 17.8 %all-gather.3 = f32[16384]{0:T(1024)S(1)} all-gather(f32[1024]{0:T(1024)S(1)} %bitcast.117), channel_id=5, replica_groups=mesh['src'=16,'tgt'=8] {'src'}, dimensions={0}, use_global_device_ids=true | all-gather | bytes 69632 | tf_op jit(solution)/shard_map/all_gather | solution.py:17
  290.0 6.1 fusion.1
  296.2 1.7 fusion.17
  297.9 17.1 %psum.88 = f32[1024]{0:T(1024)S(1)} all-reduce(f32[1024]{0:T(1024)S(1)} %add.42), channel_id=1, replica_groups=mesh['src'=16,'tgt'=8] {'tgt'}, use_global_device_ids=true, to_apply=%region_9.0 | all-reduce | flops 1024 | bytes 8192 | tf_op jit(solution)/shard_map/psum | solution.py:13
  316.0 20.8 %all-gather.5 = f32[16384]{0:T(1024)S(1)} all-gather(f32[1024]{0:T(1024)S(1)} %bitcast.124), channel_id=7, replica_groups=mesh['src'=16,'tgt'=8] {'src'}, dimensions={0}, use_global_device_ids=true | all-gather | bytes 69632 | tf_op jit(solution)/shard_map/all_gather | solution.py:17
  336.8 1.7 fusion.19
  338.6 15.5 %psum.83 = f32[1024]{0:T(1024)S(1)} all-reduce(f32[1024]{0:T(1024)S(1)} %bitcast.132), channel_id=1, replica_groups=mesh['src'=16,'tgt'=8] {'tgt'}, use_global_device_ids=true, to_apply=%region_12.0 | all-reduce | flops 1024 | bytes 8192 | tf_op jit(solution)/shard_map/psum | solution.py:13
  355.0 20.9 %all-gather.6 = f32[16384]{0:T(1024)S(1)} all-gather(f32[1024]{0:T(1024)S(1)} %bitcast.125), channel_id=8, replica_groups=mesh['src'=16,'tgt'=8] {'src'}, dimensions={0}, use_global_device_ids=true | all-gather | bytes 69632 | tf_op jit(solution)/shard_map/all_gather | solution.py:17
  375.9 1.7 fusion.21
  377.7 17.7 %psum.84 = f32[1024]{0:T(1024)S(1)} all-reduce(f32[1024]{0:T(1024)S(1)} %bitcast.133), channel_id=1, replica_groups=mesh['src'=16,'tgt'=8] {'tgt'}, use_global_device_ids=true, to_apply=%region_14.0 | all-reduce | flops 1024 | bytes 8192 | tf_op jit(solution)/shard_map/psum | solution.py:13
  396.3 20.2 %all-gather.7 = f32[16384]{0:T(1024)S(1)} all-gather(f32[1024]{0:T(1024)S(1)} %bitcast.126), channel_id=9, replica_groups=mesh['src'=16,'tgt'=8] {'src'}, dimensions={0}, use_global_device_ids=true | all-gather | bytes 69632 | tf_op jit(solution)/shard_map/all_gather | solution.py:17
  418.4 15.8 %psum.85 = f32[1024]{0:T(1024)S(1)} all-reduce(f32[1024]{0:T(1024)S(1)} %bitcast.127), channel_id=1, replica_groups=mesh['src'=16,'tgt'=8] {'tgt'}, use_global_device_ids=true, to_apply=%region_16.0 | all-reduce | flops 1024 | bytes 8192 | tf_op jit(solution)/shard_map/psum | solution.py:13
  434.3 6.2 fusion
  441.9 3.5 convolution_multiply_fusion.1
  447.0 5.0 convolution_multiply_fusion
  452.0 88.6 %all-reduce.3.cloned.1.call-done = f32[1024,768]{1,0:T(8,128)} async-done(((f32[1024,768]{1,0:T(8,128)}), f32[1024,768]{1,0:T(8,128)}) %all-reduce.3.cloned.1.call-update) | async-done | bytes 3145744 | tf_op jit(solution)/shard_map/psum | solution.py:92
  540.6 1.8 constant_dynamic-slice_fusion.1
  542.3 129.1 %all-reduce.5.cloned.1.call-done = f32[1024,768]{1,0:T(8,128)} async-done(((f32[1024,768]{1,0:T(8,128)}), f32[1024,768]{1,0:T(8,128)}) %all-reduce.5.cloned.1.call-update) | async-done | bytes 3145744 | tf_op jit(solution)/shard_map/psum | solution.py:93
  (64 shorter events, 18.2 us)
Async XLA Ops:
  7.2 56.0 %all-gather.11.cloned.1.call-start = ((), (), s32[]{:S(2)}) async-start(), calls=%async_computation | async-start | bytes 1769472 | tf_op jit(solution)/shard_map/all_gather | solution.py:30
  7.9 91.1 %all-gather.13.cloned.1.call-start = ((), (), s32[]{:S(2)}) async-start(), calls=%async_computation.1 | async-start | bytes 1671168 | tf_op jit(solution)/shard_map/all_gather | solution.py:31
  8.6 531.9 %all-reduce.3.cloned.1.call-start = ((), (), s32[]{:S(2)}) async-start(), calls=%async_computation.2 | async-start | bytes 6291456 | tf_op jit(solution)/shard_map/psum | solution.py:92
  104.6 21.9 %copy-start.2 = (f32[1024]{0:T(1024)S(1)}, f32[1024]{0:T(1024)}, u32[]{:S(2)}) copy-start(f32[1024]{0:T(1024)} %param.6) | copy-start | bytes 12292
  104.6 44.2 %copy-start.3 = (f32[1024]{0:T(1024)S(1)}, f32[1024]{0:T(1024)}, u32[]{:S(2)}) copy-start(f32[1024]{0:T(1024)} %param.7) | copy-start | bytes 12292
  434.3 7.6 %copy-start.4 = (bf16[1024,768]{1,0:T(8,128)(2,1)S(1)}, bf16[1024,768]{1,0:T(8,128)(2,1)}, u32[]{:S(2)}) copy-start(bf16[1024,768]{1,0:T(8,128)(2,1)} %all-gather.13.cloned.1.call-done) | copy-start | bytes 4718596
  440.5 1.3 copy-start
  445.4 1.6 copy-start.1
  445.4 226.0 %all-reduce.5.cloned.1.call-start = ((), (), s32[]{:S(2)}) async-start(), calls=%async_computation.3 | async-start | bytes 6291456 | tf_op jit(solution)/shard_map/psum | solution.py:93
Sparse Core Ops, SparseCore 0:
  10.3 52.8 all-gather.10
  64.9 34.0 all-gather.12
  445.5 94.9 all-reduce.2
  542.9 128.4 all-reduce.4
